TPU v7x, 128 devices: a whole 4x4x4 slice. The times are simulated.
128 devices in a mesh: req: 16 (over y, z), mlp: 8 (over x, core).
Axes of the slice: x: 4, y: 4, z: 4, core: 2. Of those that a mesh axis runs over, the one named last changes fastest.
Arguments:
- tokens: bfloat16 [32768, 1536], P(('req', 'mlp')), may hold values from -6 to 6
- attn_gain: float32 [1536], replicated, may hold values from 0.1 to 1.9
- w_query: bfloat16 [1536, 1536], replicated, may hold values from -0.15625 to 0.15625
- w_keyval: bfloat16 [1536, 256], replicated, may hold values from -0.15625 to 0.15625
- w_out: bfloat16 [1536, 1536], replicated, may hold values from -0.15625 to 0.15625
- ffn_gain: float32 [1536], replicated, may hold values from 0.1 to 1.9
- w_gate: bfloat16 [1536, 4608], P('req', 'mlp'), may hold values from -0.15625 to 0.15625
- w_up: bfloat16 [1536, 4608], P('req', 'mlp'), may hold values from -0.15625 to 0.15625
- w_down: bfloat16 [1536, 4608], P('req', 'mlp'), may hold values from -0.09375 to 0.09375
- prefix_kv: bfloat16 [2, 128, 512, 256], P(None, 'req'), may hold values from -60 to 60, as said below
- own_prefix: bfloat16 [16, 512, 256], P('req'), may hold values from -60 to 60, as said below
- leaf_parent: int32 [16], replicated, may hold values from 0 to 127
- node_parent: int32 [128], replicated, may hold values from 0 to 127
- seg_lengths: int32 [3, 128], replicated, may hold values from 1 to 512
Outputs:
- layer_out: bfloat16 [32768, 1536], P(('req', 'mlp'))
Inputs may be any that keep to these rules, and one draw needn't show every extreme that they name: `prefix_kv`: columns below 128 are keys, the rest values. `own_prefix`: columns below 128 are keys, the rest values.
All inputs are finite; a program needn't handle non-finite values.
Results may differ from a plain program's by a relative error of at most 0.018.
Values may be sent and summed in bfloat16 or wider, within the bound.
No kernel may reach another device: no remote copies, remote signals or barrier semaphores. Data moves between devices by JAX's collectives and lax.ppermute only.
A program may use at most 192 MiB of HBM per device.

v0:
```python
import jax
import jax.numpy as jnp
from jax import lax
from jax.sharding import PartitionSpec as P

HEADS = 12
HD = 128
WINDOW = 1024
EPS = 1e-06


def rms_scale(values, gain):
    wide = values.astype(jnp.float32)
    return wide * lax.rsqrt(jnp.mean(wide * wide, axis=-1, keepdims=True) + EPS) * gain


def rotate(values, where_at):
    half_dim = values.shape[-1] // 2
    freqs = 10000.0 ** (-jnp.arange(half_dim, dtype=jnp.float32) / half_dim)
    angles = where_at.astype(jnp.float32)[:, None] * freqs[None, :]
    cosine = jnp.cos(angles)[:, None, :]
    sine = jnp.sin(angles)[:, None, :]
    first = values[..., :half_dim]
    second = values[..., half_dim:]
    return jnp.concatenate([first * cosine - second * sine, first * sine + second * cosine], -1)


def attend(queries, piece, key_at, key_live, query_at):
    scores = jnp.einsum("thd,kd->thk", queries, piece[:, :HD], preferred_element_type=jnp.float32)
    spacing = query_at[:, None] - key_at[None, :]
    allowed = (key_live[None, :] & (spacing >= 0) & (spacing < WINDOW))[:, None, :]
    top = jnp.max(jnp.where(allowed, scores, -jnp.inf), axis=-1)
    safe_top = jnp.where(jnp.isfinite(top), top, 0.0)
    weights = jnp.where(allowed, jnp.exp(scores - safe_top[..., None]), 0.0)
    mixed = jnp.einsum(
        "thk,kd->thd",
        weights.astype(jnp.bfloat16),
        piece[:, HD:],
        preferred_element_type=jnp.float32,
    )
    return (top, jnp.sum(weights, axis=-1), mixed)


def combine(first, second):
    top = jnp.maximum(first[0], second[0])
    safe_top = jnp.where(jnp.isfinite(top), top, 0.0)
    scale_first = jnp.exp(first[0] - safe_top)
    scale_second = jnp.exp(second[0] - safe_top)
    denom = first[1] * scale_first + second[1] * scale_second
    mixed = first[2] * scale_first[..., None] + second[2] * scale_second[..., None]
    return (top, denom, mixed)


def body(
    tokens,
    attn_gain,
    w_query,
    w_keyval,
    w_out,
    ffn_gain,
    w_gate,
    w_up,
    w_down,
    prefix_kv,
    own_prefix,
    leaf_parent,
    node_parent,
    seg_lengths,
):
    tok_rows = tokens.shape[0]
    requests = lax.axis_size("req")
    mine = lax.axis_index("req")
    position_group = lax.axis_index("mlp")
    node_dev = prefix_kv.shape[1]
    seg_slot = prefix_kv.shape[2]
    leaf = leaf_parent[mine]
    upper = node_parent[leaf]
    len_zero = seg_lengths[0, upper]
    len_one = seg_lengths[1, leaf]
    len_two = seg_lengths[2, mine]
    total = len_zero + len_one + len_two
    query_at = total + position_group * tok_rows + jnp.arange(tok_rows, dtype=jnp.int32)
    normed = rms_scale(tokens, attn_gain).astype(jnp.bfloat16)
    query_full = jnp.dot(normed, w_query, preferred_element_type=jnp.float32).reshape(
        tok_rows, HEADS, HD
    )
    queries = (rotate(query_full, query_at) * HD ** (-0.5)).astype(jnp.bfloat16)
    keyval_full = jnp.dot(normed, w_keyval, preferred_element_type=jnp.float32)
    new_keys = rotate(keyval_full[:, None, :HD], query_at)[:, 0].astype(jnp.bfloat16)
    new_vals = keyval_full[:, HD:].astype(jnp.bfloat16)
    new_keyval = jnp.concatenate([new_keys, new_vals], 1)
    start_state = (
        jnp.full((tok_rows, HEADS), -jnp.inf, jnp.float32),
        jnp.zeros((tok_rows, HEADS), jnp.float32),
        jnp.zeros((tok_rows, HEADS, HD), jnp.float32),
    )
    piece = lax.all_gather(new_keyval, "mlp", axis=0, tiled=True)
    piece_at = total + jnp.arange(piece.shape[0], dtype=jnp.int32)
    live = jnp.ones((piece.shape[0],), dtype=bool)
    own_state = combine(start_state, attend(queries, piece, piece_at, live, query_at))
    level_zero = node_parent[leaf_parent]
    wanted = jnp.stack([level_zero, leaf_parent], 1)
    owned = wanted // node_dev == mine
    local_slot = wanted % node_dev
    picker = (
        (local_slot[:, :, None] == jnp.arange(node_dev, dtype=jnp.int32)[None, None, :])
        & owned[:, :, None]
    ).astype(jnp.bfloat16)
    owners = wanted[mine] // node_dev
    from_owner = (jnp.arange(requests, dtype=jnp.int32)[:, None] == owners[None, :]).astype(
        jnp.bfloat16
    )
    outgoing = jnp.einsum(
        "rln,lnsc->rlsc", picker, prefix_kv, preferred_element_type=jnp.float32
    ).astype(jnp.bfloat16)
    arrived = lax.all_to_all(outgoing, "req", split_axis=0, concat_axis=0, tiled=True)
    levels = jnp.einsum(
        "rl,rlsc->lsc", from_owner, arrived, preferred_element_type=jnp.float32
    ).astype(jnp.bfloat16)
    offsets = jnp.arange(seg_slot, dtype=jnp.int32)
    cached = jnp.concatenate([levels[0], levels[1], own_prefix[0]], 0)
    cached_at = jnp.concatenate([offsets, len_zero + offsets, len_zero + len_one + offsets], 0)
    cached_live = jnp.concatenate([offsets < len_zero, offsets < len_one, offsets < len_two], 0)
    merged = combine(own_state, attend(queries, cached, cached_at, cached_live, query_at))
    context = (merged[2] / merged[1][..., None]).reshape(tok_rows, HEADS * HD).astype(jnp.bfloat16)
    attn_out = jnp.dot(context, w_out, preferred_element_type=jnp.float32)
    resid = (tokens.astype(jnp.float32) + attn_out).astype(jnp.bfloat16)
    ffn_in = rms_scale(resid, ffn_gain).astype(jnp.bfloat16)
    all_rows = lax.all_gather(ffn_in, "mlp", axis=0, tiled=True)
    gate_full, up_full, down_full = (
        lax.all_gather(w_gate, "req", axis=0, tiled=True),
        lax.all_gather(w_up, "req", axis=0, tiled=True),
        lax.all_gather(w_down, "req", axis=0, tiled=True),
    )
    gate = jnp.dot(all_rows, gate_full, preferred_element_type=jnp.float32)
    upward = jnp.dot(all_rows, up_full, preferred_element_type=jnp.float32)
    hidden = (jax.nn.gelu(gate, approximate=True) * upward).astype(jnp.bfloat16)
    summed = lax.psum_scatter(
        lax.dot_general(
            hidden, down_full, (((1,), (1,)), ((), ())), preferred_element_type=jnp.float32
        ).astype(jnp.bfloat16),
        "mlp",
        scatter_dimension=0,
        tiled=True,
    ).astype(jnp.float32)
    return (resid.astype(jnp.float32) + summed).astype(jnp.bfloat16)


def solution(mesh):
    return jax.shard_map(
        body,
        mesh=mesh,
        in_specs=(
            P(("req", "mlp"), None),
            P(),
            P(),
            P(),
            P(),
            P(),
            P("req", "mlp"),
            P("req", "mlp"),
            P("req", "mlp"),
            P(None, "req", None, None),
            P("req", None, None),
            P(),
            P(),
            P(),
        ),
        out_specs=P(("req", "mlp"), None),
        check_vma=False,
    )
```

profile of v0, /device:TPU:1, one launch (start us, length us, event | category | flops | bytes accessed | tf_op | source)
XLA Modules:
  0.0 438.2 jit_solution(3613787128685627271)
XLA Ops:
  6.6 1.3 dynamic_slice.18
  9.8 1.2 dynamic_slice.19
  12.4 1.4 fusion.25
  13.8 1.7 fusion.35
  16.1 1.5 constant_dynamic-slice_fusion
  19.8 0.7 pad_maximum_fusion.1
  20.5 0.7 compare_select_fusion
  21.9 7.2 %convert_bitcast_fusion = bf16[16,2,512,256]{3,0,2,1:T(8,128)(2,1)} fusion(bf16[2,8,512,256]{3,2,1,0:T(8,128)(2,1)} %param.23, s32[16,2]{0,1:T(2,128)S(1)} %get-tuple-element.24, pred[16,2]{0,1:T(4,128)(4,1)S(1)} %fusion.54), kind=kOutput, calls=%fused_computation.15 | convolution fusion | flops 71303680 | bytes 12583072 | tf_op jit(solution)/shard_map/rln,lnsc->rlsc/dot_general | solution.py:113
  29.1 9.6 %copy.33 = bf16[16,2,512,256]{3,2,1,0:T(8,128)(2,1)} copy(bf16[16,2,512,256]{3,0,2,1:T(8,128)(2,1)} %convert_bitcast_fusion) | data formatting | bytes 16777216 | tf_op jit(solution)/shard_map/convert_element_type | solution.py:115
  38.8 8.9 %all-to-all-start = ((bf16[16,2,512,256]{3,2,1,0:T(8,128)(2,1)}), bf16[16,2,512,256]{3,2,1,0:T(8,128)(2,1)}, u32[]{:S(2)}, u32[]{:S(2)}) async-start(bf16[16,2,512,256]{3,2,1,0:T(8,128)(2,1)} %copy.33), calls=%async_computation | async-start | bytes 16777216 | tf_op jit(solution)/shard_map/all_to_all | solution.py:116
  47.7 0.7 all-gather.10.cloned.1.call-update
  48.8 4.3 fusion.37
  53.8 1.6 copy.44
  56.4 1.3 iota_compare_fusion.2
  58.8 1.9 multiply_subtract_fusion
  62.3 11.8 %select_reduce_fusion = (f32[256,12]{0,1:T(8,128)S(1)}, f32[256,12,2048]{2,0,1:T(8,128)}) fusion(pred[256,2048]{1,0:T(8,128)(4,1)S(1)} %fusion.24, bf16[256,12,128]{2,0,1:T(8,128)(2,1)S(1)} %fusion.28, bf16[2048,256]{0,1:T(8,128)(2,1)} %all-gather.6.cloned.1.call-done), kind=kOutput, calls=%fused_computation.2 | convolution fusion | flops 1623192576 | bytes 27013120 | tf_op jit(solution)/shard_map/thd,kd->thk/dot_general | solution.py:29
  74.2 11.3 %fusion = f32[256,12]{0,1:T(8,128)S(1)} fusion(f32[256,12,2048]{2,0,1:T(8,128)} %get-tuple-element.27, f32[256,12]{0,1:T(8,128)S(1)} %get-tuple-element.18, pred[256,2048]{1,0:T(8,128)(4,1)S(1)} %fusion.24), kind=kLoop, calls=%fused_computation.3 | loop fusion | flops 18871296 | bytes 25714688 | tf_op jit(solution)/shard_map/reduce_sum | solution.py:41
  85.5 11.8 %fusion.4 = f32[256,12,128]{0,2,1:T(8,128)} fusion(f32[256,12,2048]{2,0,1:T(8,128)} %get-tuple-element.27, f32[256,12]{0,1:T(8,128)S(1)} %get-tuple-element.18, pred[256,2048]{1,0:T(8,128)(4,1)S(1)} %fusion.24, bf16[2048,256]{0,1:T(8,128)(2,1)S(1)} %copy-done.5), kind=kOutput, calls=%fused_computation.9 | convolution fusion | flops 1629487104 | bytes 27803648 | tf_op jit(solution)/shard_map/thk,kd->thd/dot_general | solution.py:35
  97.3 97.6 %all-to-all-done = bf16[16,2,512,256]{3,2,1,0:T(8,128)(2,1)} async-done(((bf16[16,2,512,256]{3,2,1,0:T(8,128)(2,1)}), bf16[16,2,512,256]{3,2,1,0:T(8,128)(2,1)}, u32[]{:S(2)}, u32[]{:S(2)}) %all-to-all-start) | async-done | bytes 8388640 | tf_op jit(solution)/shard_map/all_to_all | solution.py:116
  194.9 8.3 %fusion.10 = bf16[2,1,512,256]{3,1,2,0:T(2,128)(2,1)S(1)} fusion(pred[16,2,1,1]{0,2,3,1:T(4,128)(4,1)S(1)} %copy.38, bf16[16,2,512,256]{3,2,1,0:T(8,128)(2,1)} %all-to-all-done), kind=kOutput, calls=%fused_computation.13 | convolution fusion | flops 8388608 | bytes 8912928 | tf_op jit(solution)/shard_map/rl,rlsc->lsc/dot_general | solution.py:117
  203.4 8.0 %select_reduce_fusion.1 = (f32[256,12]{0,1:T(8,128)S(1)}, f32[256,12,1536]{2,0,1:T(8,128)}) fusion(pred[256,1536]{1,0:T(8,128)(4,1)S(1)} %fusion.30, bf16[256,12,128]{2,0,1:T(8,128)(2,1)S(1)} %fusion.28, bf16[1536,256]{1,0:T(8,128)(2,1)S(1)} %pad_maximum_fusion), kind=kOutput, calls=%fused_computation.6 | convolution fusion | flops 1217393664 | bytes 20459520 | tf_op jit(solution)/shard_map/thd,kd->thk/dot_general | solution.py:29
  211.5 10.5 %fusion.2 = f32[256,12]{0,1:T(8,128)S(1)} fusion(f32[256,12,1536]{2,0,1:T(8,128)} %get-tuple-element.29, f32[256,12]{0,1:T(8,128)S(1)} %is-finite_select_fusion, pred[256,1536]{1,0:T(8,128)(4,1)S(1)} %fusion.30), kind=kLoop, calls=%fused_computation.7 | loop fusion | flops 14152704 | bytes 19292160 | tf_op jit(solution)/shard_map/reduce_sum | solution.py:41
  222.0 8.7 %divide_convert_fusion = bf16[256,12,128]{0,2,1:T(8,128)(2,1)S(1)} fusion(f32[256,12,128]{0,2,1:T(8,128)} %fusion.4, f32[256,12,1536]{2,0,1:T(8,128)} %get-tuple-element.29, f32[256,12]{0,1:T(8,128)S(1)} %is-finite_select_fusion, pred[256,1536]{1,0:T(8,128)(4,1)S(1)} %fusion.30, f32[256,12]{0,1:T(8,128)S(1)} %get-tuple-element.5, ...), kind=kOutput, calls=%fused_computation.46 | convolution fusion | flops 1224867840 | bytes 22118400 | tf_op jit(solution)/shard_map/thk,kd->thd/dot_general | solution.py:35
  230.8 1.5 multiply_reduce_fusion
  232.3 1.1 multiply_convert_fusion
  234.7 44.8 %all-gather.8.cloned.1.call-done = bf16[2048,1536]{1,0:T(8,128)(2,1)} async-done(((bf16[256,1536]{1,0:T(8,128)(2,1)}), bf16[2048,1536]{1,0:T(8,128)(2,1)}) %all-gather.8.cloned.1.call-update) | async-done | bytes 6291472 | tf_op jit(solution)/shard_map/all_gather | solution.py:129
  279.4 9.3 %fusion.63 = f32[2048,576]{0,1:T(8,128)} fusion(bf16[2048,1536]{1,0:T(8,128)(2,1)} %all-gather.8.cloned.1.call-done, bf16[1536,576]{1,0:T(8,128)(2,1)} %all-gather.10.cloned.1.call-done), kind=kOutput, calls=%fused_computation.133 | convolution fusion | flops 3623878656 | bytes 12779520 | tf_op jit(solution)/shard_map/dot_general | solution.py:135
  288.8 36.4 %all-gather.14.cloned.1.call-done = bf16[1536,576]{1,0:T(8,128)(2,1)} async-done(((bf16[96,576]{1,0:T(8,128)(2,1)}), bf16[1536,576]{1,0:T(8,128)(2,1)}) %all-gather.14.cloned.1.call-update) | async-done | bytes 1769488 | tf_op jit(solution)/shard_map/all_gather | solution.py:133
  325.2 46.1 %all-gather.12.cloned.1.call-done = bf16[1536,576]{1,0:T(8,128)(2,1)} async-done(((bf16[96,576]{1,0:T(8,128)(2,1)}), bf16[1536,576]{1,0:T(8,128)(2,1)}) %all-gather.12.cloned.1.call-update) | async-done | bytes 1769488 | tf_op jit(solution)/shard_map/all_gather | solution.py:132
  371.2 15.6 %convolution_convert_fusion = bf16[2048,1536]{1,0:T(8,128)(2,1)} fusion(bf16[1536,576]{1,0:T(8,128)(2,1)} %all-gather.14.cloned.1.call-done, f32[2048,576]{0,1:T(8,128)} %fusion.63, bf16[2048,1536]{1,0:T(8,128)(2,1)} %all-gather.8.cloned.1.call-done, bf16[1536,576]{1,0:T(8,128)(2,1)} %all-gather.12.cloned.1.call-done), kind=kOutput, calls=%fused_computation.16 | convolution fusion | flops 7262699520 | bytes 20840448 | tf_op jit(solution)/shard_map/dot_general | solution.py:139
  386.8 42.0 %reduce-scatter.2.cloned.1.call-done = bf16[256,1536]{1,0:T(8,128)(2,1)} async-done(((bf16[2048,1536]{1,0:T(8,128)(2,1)}), bf16[256,1536]{1,0:T(8,128)(2,1)}) %reduce-scatter.2.cloned.1.call-update) | async-done | bytes 786448 | tf_op jit(solution)/shard_map/reduce_scatter | solution.py:138
  428.9 2.2 add_convert_fusion
  (72 shorter events, 7.3 us)
Async XLA Ops:
  6.5 7.2 %copy-start = (bf16[1536,256]{1,0:T(8,128)(2,1)S(1)}, bf16[1536,256]{1,0:T(8,128)(2,1)}, u32[]{:S(2)}) copy-start(bf16[1536,256]{1,0:T(8,128)(2,1)} %param.17) | copy-start | bytes 2359300
  6.5 15.3 %copy-start.8 = (s32[16]{0:T(128)S(1)}, s32[16]{0:T(128)}, u32[]{:S(2)}) copy-start(s32[16]{0:T(128)} %param.25) | copy-start | bytes 196
  6.5 14.7 %copy-start.2 = (s32[128]{0:T(128)S(1)}, s32[128]{0:T(128)}, u32[]{:S(2)}) copy-start(s32[128]{0:T(128)} %param.26) | copy-start | bytes 1540
  6.5 55.8 %all-gather.6.cloned.1.call-start = ((), (), s32[]{:S(2)}) async-start(), calls=%async_computation.2 | async-start | bytes 1179648 | tf_op jit(solution)/shard_map/all_gather | solution.py:97
  38.8 10.0 %copy-start.3 = (bf16[256,1536]{1,0:T(8,128)(2,1)S(1)}, bf16[256,1536]{1,0:T(8,128)(2,1)}, u32[]{:S(2)}) copy-start(bf16[256,1536]{1,0:T(8,128)(2,1)} %param.14) | copy-start | bytes 2359300
  38.8 10.0 %copy-start.9 = (f32[1536]{0:T(1024)S(1)}, f32[1536]{0:T(1024)}, u32[]{:S(2)}) copy-start(f32[1536]{0:T(1024)} %param.15) | copy-start | bytes 18436
  38.8 156.1 %all-to-all-start = ((bf16[16,2,512,256]{3,2,1,0:T(8,128)(2,1)}), bf16[16,2,512,256]{3,2,1,0:T(8,128)(2,1)}, u32[]{:S(2)}, u32[]{:S(2)}) async-start(bf16[16,2,512,256]{3,2,1,0:T(8,128)(2,1)} %copy.33), calls=%async_computation | async-start | bytes 16777216 | tf_op jit(solution)/shard_map/all_to_all | solution.py:116
  47.7 187.0 %all-gather.10.cloned.1.call-start = ((), (), s32[]{:S(2)}) async-start(), calls=%async_computation.4 | async-start | bytes 2088960 | tf_op jit(solution)/shard_map/all_gather | solution.py:131
  48.4 231.0 %all-gather.8.cloned.1.call-start = ((), (), s32[]{:S(2)}) async-start(), calls=%async_computation.3 | async-start | bytes 7077888 | tf_op jit(solution)/shard_map/all_gather | solution.py:129
  74.2 11.4 %copy-start.5 = (bf16[2048,256]{0,1:T(8,128)(2,1)S(1)}, bf16[2048,256]{0,1:T(8,128)(2,1)}, u32[]{:S(2)}) copy-start(bf16[2048,256]{0,1:T(8,128)(2,1)} %all-gather.6.cloned.1.call-done) | copy-start | bytes 3145732
  97.3 106.0 %copy-start.6 = (bf16[1,512,256]{2,1,0:T(8,128)(2,1)S(1)}, bf16[1,512,256]{2,1,0:T(8,128)(2,1)}, u32[]{:S(2)}) copy-start(bf16[1,512,256]{2,1,0:T(8,128)(2,1)} %param.24) | copy-start | bytes 786436
  211.5 19.3 %slice-start = ((s8[4718592]{0:T(1024)(128)(4,1)}), s8[524288]{0:T(1024)(128)(4,1)S(1)}, s32[]{:S(2)}) async-start(s8[4718592]{0:T(1024)(128)(4,1)} %bitcast.58), calls=%async_computation.8 | async-start | bytes 1048576
  222.0 8.8 %slice-start.1 = ((s8[4718592]{0:T(1024)(128)(4,1)}), s8[4194304]{0:T(1024)(128)(4,1)S(1)}, s32[]{:S(2)}) async-start(s8[4718592]{0:T(1024)(128)(4,1)} %bitcast.58), calls=%async_computation.9 | async-start | bytes 8388608
  222.0 8.8 %copy-start.4 = (bf16[256,1536]{1,0:T(8,128)(2,1)S(1)}, bf16[256,1536]{1,0:T(8,128)(2,1)}, u32[]{:S(2)}) copy-start(bf16[256,1536]{1,0:T(8,128)(2,1)} %param.14) | copy-start | bytes 2359300
  230.8 1.5 copy-start.7
  233.4 91.7 %all-gather.14.cloned.1.call-start = ((), (), s32[]{:S(2)}) async-start(), calls=%async_computation.6 | async-start | bytes 2088960 | tf_op jit(solution)/shard_map/all_gather | solution.py:133
  234.0 137.2 %all-gather.12.cloned.1.call-start = ((), (), s32[]{:S(2)}) async-start(), calls=%async_computation.5 | async-start | bytes 2088960 | tf_op jit(solution)/shard_map/all_gather | solution.py:132
  234.6 194.3 %reduce-scatter.2.cloned.1.call-start = ((), (), s32[]{:S(2)}) async-start(), calls=%async_computation.7 | async-start | bytes 7077888 | tf_op jit(solution)/shard_map/reduce_scatter | solution.py:138
  386.8 44.3 %copy-start.1 = (bf16[1536,256]{1,0:T(8,128)(2,1)S(1)}, bf16[1536,256]{1,0:T(8,128)(2,1)}, u32[]{:S(2)}) copy-start(bf16[1536,256]{1,0:T(8,128)(2,1)} %param.17) | copy-start | bytes 2359300
Sparse Core Ops, SparseCore 0:
  20.7 26.9 all-gather.5
  50.7 139.0 all-gather.9
  233.6 45.8 all-gather.7
  281.5 43.6 all-gather.13
  327.2 43.9 all-gather.11
  387.0 41.8 reduce-scatter.1
where the time goes:
time: 444 us; the launch traced here: 438 us
  waiting for transfers between devices  269 us (61%)
  matrix products  88.4 us (20%)
  other arithmetic  35 us (8%)
  between operations  19.9 us (4%)
  local copies, waits for them, and re-layouts  16.9 us (4%)
  starting transfers between devices  9.38 us (2%)
    all_to_all x1, waiting for transfers between devices, body(): lax.all_to_all(outgoing, 'req', split_axis=0, concat_axis=0, tiled=True)  97.6 us
    all_gather x1, waiting for transfers between devices, body(): lax.all_gather(w_up, 'req', axis=0, tiled=True)  46.1 us
    all_gather x1, waiting for transfers between devices, body(): all_rows = lax.all_gather(ffn_in, 'mlp', axis=0, tiled=True)  44.8 us
    reduce_scatter x1, waiting for transfers between devices, body(): lax.psum_scatter(lax.dot_general(hidden, down_full, (((1,), (1,)), ((), (...  42 us
    all_gather x1, waiting for transfers between devices, body(): lax.all_gather(w_down, 'req', axis=0, tiled=True)  36.4 us
    reduce_sum x2, other arithmetic, attend(): return (top, jnp.sum(weights, axis=-1), mixed)  21.8 us
    dot_general x2, matrix products, attend(): jnp.einsum('thk,kd->thd', weights.astype(jnp.bfloat16), piece[:, HD:], pr...  20.5 us
    dot_general x2, matrix products, attend(): jnp.einsum('thd,kd->thk', queries, piece[:, :HD], preferred_element_type=...  19.9 us
  transfers between devices with their start and end apart: 7, of which 5 were waited for; matrix products, arithmetic and copies ran while one was open for 26% of the time, Pallas kernels for 0%

commit v1 on v0

--- a/solution.py
+++ b/solution.py
@@ -129,7 +129,9 @@
     all_rows = lax.all_gather(ffn_in, "mlp", axis=0, tiled=True)
     gate_full, up_full, down_full = (
         lax.all_gather(w_gate, "req", axis=0, tiled=True),
-        lax.all_gather(w_up, "req", axis=0, tiled=True),
+        jnp.concatenate(
+            lax.all_to_all(jnp.stack([w_up] * lax.axis_size("req")), "req", 0, 0), axis=0
+        ),
         lax.all_gather(w_down, "req", axis=0, tiled=True),
     )
     gate = jnp.dot(all_rows, gate_full, preferred_element_type=jnp.float32)

time: 444 us -> 398 us (0.90)
  waiting for transfers between devices: 269 us -> 213 us
  starting transfers between devices: 9.38 us -> 17.8 us
    all_gather x1 -> x0, waiting for transfers between devices: 46.1 us -> none  [body(): lax.all_gather(w_up, 'req', axis=0, tiled=True)]
    all_gather x1, waiting for transfers between devices: 44.8 us -> 35.4 us  [body(): all_rows = lax.all_gather(ffn_in, 'mlp', axis=0, tiled=True)]
    all_to_all x0 -> x1, starting transfers between devices: none -> 8.5 us  [body(): lax.all_to_all(jnp.stack([w_up] * lax.axis_size('req')), 'req', 0, 0)]
  transfers between devices with their start and end apart: 7 -> 7, of which waited for: 5 -> 4; matrix products, arithmetic and copies ran while one was open for 26% -> 30% of each run, Pallas kernels for 0% -> 0%
where the time goes in v1:
time: 398 us; the launch traced here: 392 us
  waiting for transfers between devices  213 us (54%)
  matrix products  88.3 us (22%)
  other arithmetic  35 us (9%)
  between operations  19.6 us (5%)
  local copies, waits for them, and re-layouts  18.4 us (5%)
  starting transfers between devices  17.8 us (4%)
    all_to_all x1, waiting for transfers between devices, body(): lax.all_to_all(outgoing, 'req', split_axis=0, concat_axis=0, tiled=True)  97.6 us
    reduce_scatter x1, waiting for transfers between devices, body(): lax.psum_scatter(lax.dot_general(hidden, down_full, (((1,), (1,)), ((), (...  42.1 us
    all_gather x1, waiting for transfers between devices, body(): lax.all_gather(w_down, 'req', axis=0, tiled=True)  36.4 us
    all_gather x1, waiting for transfers between devices, body(): all_rows = lax.all_gather(ffn_in, 'mlp', axis=0, tiled=True)  35.4 us
    reduce_sum x2, other arithmetic, attend(): return (top, jnp.sum(weights, axis=-1), mixed)  21.8 us
    dot_general x2, matrix products, attend(): jnp.einsum('thk,kd->thd', weights.astype(jnp.bfloat16), piece[:, HD:], pr...  20.5 us
    dot_general x2, matrix products, attend(): jnp.einsum('thd,kd->thk', queries, piece[:, :HD], preferred_element_type=...  19.9 us
    dot_general x1, matrix products, body(): lax.dot_general(hidden, down_full, (((1,), (1,)), ((), ())), preferred_el...  15.6 us
  transfers between devices with their start and end apart: 7, of which 4 were waited for; matrix products, arithmetic and copies ran while one was open for 30% of the time, Pallas kernels for 0%

profile of v1, /device:TPU:1, one launch (start us, length us, event | category | flops | bytes accessed | tf_op | source)
XLA Modules:
  0.0 391.8 jit_solution(3532366713728168644)
XLA Ops:
  6.6 1.3 dynamic_slice.18
  9.8 1.2 dynamic_slice.19
  12.4 1.4 fusion.25
  13.8 1.7 fusion.35
  16.1 1.5 constant_dynamic-slice_fusion
  19.8 0.7 pad_maximum_fusion.1
  21.9 7.2 %convert_bitcast_fusion = bf16[16,2,512,256]{3,0,2,1:T(8,128)(2,1)} fusion(bf16[2,8,512,256]{3,2,1,0:T(8,128)(2,1)} %param.23, s32[16,2]{0,1:T(2,128)S(1)} %get-tuple-element.24, pred[16,2]{0,1:T(4,128)(4,1)S(1)} %fusion.54), kind=kOutput, calls=%fused_computation.15 | convolution fusion | flops 71303680 | bytes 12583072 | tf_op jit(solution)/shard_map/rln,lnsc->rlsc/dot_general | solution.py:113
  29.1 9.6 %copy.33 = bf16[16,2,512,256]{3,2,1,0:T(8,128)(2,1)} copy(bf16[16,2,512,256]{3,0,2,1:T(8,128)(2,1)} %convert_bitcast_fusion) | data formatting | bytes 16777216 | tf_op jit(solution)/shard_map/convert_element_type | solution.py:115
  38.8 8.9 %all-to-all-start = ((bf16[16,2,512,256]{3,2,1,0:T(8,128)(2,1)}), bf16[16,2,512,256]{3,2,1,0:T(8,128)(2,1)}, u32[]{:S(2)}, u32[]{:S(2)}) async-start(bf16[16,2,512,256]{3,2,1,0:T(8,128)(2,1)} %copy.33), calls=%async_computation | async-start | bytes 16777216 | tf_op jit(solution)/shard_map/all_to_all | solution.py:116
  47.7 0.7 all-gather.9.cloned.1.call-update
  48.8 4.3 %fusion.37 = f32[256,1536]{0,1:T(8,128)S(1)} fusion(bf16[1536,1536]{1,0:T(8,128)(2,1)} %param.16, bf16[256,1536]{1,0:T(8,128)(2,1)S(1)} %copy-done.3, f32[1536]{0:T(1024)S(1)} %copy-done.10, f32[256]{0:T(256)S(1)} %add_rsqrt_fusion.1), kind=kOutput, calls=%fused_computation.62 | convolution fusion | flops 1209532416 | bytes 7085056 | tf_op jit(solution)/shard_map/dot_general | solution.py:84
  53.8 1.6 copy.44
  56.4 1.3 iota_compare_fusion.2
  58.8 1.9 multiply_subtract_fusion
  62.3 11.8 %select_reduce_fusion = (f32[256,12]{0,1:T(8,128)S(1)}, f32[256,12,2048]{2,0,1:T(8,128)}) fusion(pred[256,2048]{1,0:T(8,128)(4,1)S(1)} %fusion.24, bf16[256,12,128]{2,0,1:T(8,128)(2,1)S(1)} %fusion.28, bf16[2048,256]{0,1:T(8,128)(2,1)} %all-gather.5.cloned.1.call-done), kind=kOutput, calls=%fused_computation.2 | convolution fusion | flops 1623192576 | bytes 27013120 | tf_op jit(solution)/shard_map/thd,kd->thk/dot_general | solution.py:29
  74.2 11.3 %fusion = f32[256,12]{0,1:T(8,128)S(1)} fusion(f32[256,12,2048]{2,0,1:T(8,128)} %get-tuple-element.27, f32[256,12]{0,1:T(8,128)S(1)} %get-tuple-element.18, pred[256,2048]{1,0:T(8,128)(4,1)S(1)} %fusion.24), kind=kLoop, calls=%fused_computation.3 | loop fusion | flops 18871296 | bytes 25714688 | tf_op jit(solution)/shard_map/reduce_sum | solution.py:41
  85.5 11.8 %fusion.4 = f32[256,12,128]{0,2,1:T(8,128)} fusion(f32[256,12,2048]{2,0,1:T(8,128)} %get-tuple-element.27, f32[256,12]{0,1:T(8,128)S(1)} %get-tuple-element.18, pred[256,2048]{1,0:T(8,128)(4,1)S(1)} %fusion.24, bf16[2048,256]{0,1:T(8,128)(2,1)S(1)} %copy-done.5), kind=kOutput, calls=%fused_computation.9 | convolution fusion | flops 1629487104 | bytes 27803648 | tf_op jit(solution)/shard_map/thk,kd->thd/dot_general | solution.py:35
  97.3 97.6 %all-to-all-done = bf16[16,2,512,256]{3,2,1,0:T(8,128)(2,1)} async-done(((bf16[16,2,512,256]{3,2,1,0:T(8,128)(2,1)}), bf16[16,2,512,256]{3,2,1,0:T(8,128)(2,1)}, u32[]{:S(2)}, u32[]{:S(2)}) %all-to-all-start) | async-done | bytes 8388640 | tf_op jit(solution)/shard_map/all_to_all | solution.py:116
  194.9 8.3 %fusion.10 = bf16[2,1,512,256]{3,1,2,0:T(2,128)(2,1)S(1)} fusion(pred[16,2,1,1]{0,2,3,1:T(4,128)(4,1)S(1)} %copy.38, bf16[16,2,512,256]{3,2,1,0:T(8,128)(2,1)} %all-to-all-done), kind=kOutput, calls=%fused_computation.13 | convolution fusion | flops 8388608 | bytes 8912928 | tf_op jit(solution)/shard_map/rl,rlsc->lsc/dot_general | solution.py:117
  203.4 8.0 %select_reduce_fusion.1 = (f32[256,12]{0,1:T(8,128)S(1)}, f32[256,12,1536]{2,0,1:T(8,128)}) fusion(pred[256,1536]{1,0:T(8,128)(4,1)S(1)} %fusion.30, bf16[256,12,128]{2,0,1:T(8,128)(2,1)S(1)} %fusion.28, bf16[1536,256]{1,0:T(8,128)(2,1)S(1)} %pad_maximum_fusion), kind=kOutput, calls=%fused_computation.6 | convolution fusion | flops 1217393664 | bytes 20459520 | tf_op jit(solution)/shard_map/thd,kd->thk/dot_general | solution.py:29
  211.5 10.5 %fusion.2 = f32[256,12]{0,1:T(8,128)S(1)} fusion(f32[256,12,1536]{2,0,1:T(8,128)} %get-tuple-element.29, f32[256,12]{0,1:T(8,128)S(1)} %is-finite_select_fusion, pred[256,1536]{1,0:T(8,128)(4,1)S(1)} %fusion.30), kind=kLoop, calls=%fused_computation.7 | loop fusion | flops 14152704 | bytes 19292160 | tf_op jit(solution)/shard_map/reduce_sum | solution.py:41
  222.0 8.7 %divide_convert_fusion = bf16[256,12,128]{0,2,1:T(8,128)(2,1)S(1)} fusion(f32[256,12,128]{0,2,1:T(8,128)} %fusion.4, f32[256,12,1536]{2,0,1:T(8,128)} %get-tuple-element.29, f32[256,12]{0,1:T(8,128)S(1)} %is-finite_select_fusion, pred[256,1536]{1,0:T(8,128)(4,1)S(1)} %fusion.30, f32[256,12]{0,1:T(8,128)S(1)} %get-tuple-element.5, ...), kind=kOutput, calls=%fused_computation.46 | convolution fusion | flops 1224867840 | bytes 22118400 | tf_op jit(solution)/shard_map/thk,kd->thd/dot_general | solution.py:35
  230.8 1.5 multiply_reduce_fusion
  232.3 1.1 multiply_convert_fusion
  234.0 1.5 stack.11
  235.5 8.5 %all-to-all-start.1 = ((bf16[16,96,576]{2,1,0:T(8,128)(2,1)}), bf16[16,96,576]{2,1,0:T(8,128)(2,1)}, u32[]{:S(2)}, u32[]{:S(2)}) async-start(bf16[16,96,576]{2,1,0:T(8,128)(2,1)} %stack.11), calls=%async_computation.1 | async-start | bytes 3932160 | tf_op jit(solution)/shard_map/all_to_all | solution.py:133
  244.1 35.4 %all-gather.7.cloned.1.call-done = bf16[2048,1536]{1,0:T(8,128)(2,1)} async-done(((bf16[256,1536]{1,0:T(8,128)(2,1)}), bf16[2048,1536]{1,0:T(8,128)(2,1)}) %all-gather.7.cloned.1.call-update) | async-done | bytes 6291472 | tf_op jit(solution)/shard_map/all_gather | solution.py:129
  279.4 9.3 %fusion.63 = f32[2048,576]{0,1:T(8,128)} fusion(bf16[2048,1536]{1,0:T(8,128)(2,1)} %all-gather.7.cloned.1.call-done, bf16[1536,576]{1,0:T(8,128)(2,1)} %all-gather.9.cloned.1.call-done), kind=kOutput, calls=%fused_computation.133 | convolution fusion | flops 3623878656 | bytes 12779520 | tf_op jit(solution)/shard_map/dot_general | solution.py:137
  288.8 36.4 %all-gather.11.cloned.1.call-done = bf16[1536,576]{1,0:T(8,128)(2,1)} async-done(((bf16[96,576]{1,0:T(8,128)(2,1)}), bf16[1536,576]{1,0:T(8,128)(2,1)}) %all-gather.11.cloned.1.call-update) | async-done | bytes 1769488 | tf_op jit(solution)/shard_map/all_gather | solution.py:135
  325.2 15.6 %convolution_convert_fusion = bf16[2048,1536]{1,0:T(8,128)(2,1)} fusion(bf16[1536,576]{1,0:T(8,128)(2,1)} %all-gather.11.cloned.1.call-done, f32[2048,576]{0,1:T(8,128)} %fusion.63, bf16[2048,1536]{1,0:T(8,128)(2,1)} %all-gather.7.cloned.1.call-done, bf16[1536,576]{1,0:T(8,128)(2,1)} %bitcast.23), kind=kOutput, calls=%fused_computation.16 | convolution fusion | flops 7262699520 | bytes 20840448 | tf_op jit(solution)/shard_map/dot_general | solution.py:141
  340.8 42.1 %reduce-scatter.2.cloned.1.call-done = bf16[256,1536]{1,0:T(8,128)(2,1)} async-done(((bf16[2048,1536]{1,0:T(8,128)(2,1)}), bf16[256,1536]{1,0:T(8,128)(2,1)}) %reduce-scatter.2.cloned.1.call-update) | async-done | bytes 786448 | tf_op jit(solution)/shard_map/reduce_scatter | solution.py:140
  382.9 2.2 add_convert_fusion
  (74 shorter events, 7.4 us)
Async XLA Ops:
  6.5 7.2 %copy-start = (bf16[1536,256]{1,0:T(8,128)(2,1)S(1)}, bf16[1536,256]{1,0:T(8,128)(2,1)}, u32[]{:S(2)}) copy-start(bf16[1536,256]{1,0:T(8,128)(2,1)} %param.17) | copy-start | bytes 2359300
  6.5 15.3 %copy-start.9 = (s32[16]{0:T(128)S(1)}, s32[16]{0:T(128)}, u32[]{:S(2)}) copy-start(s32[16]{0:T(128)} %param.25) | copy-start | bytes 196
  6.5 14.7 %copy-start.2 = (s32[128]{0:T(128)S(1)}, s32[128]{0:T(128)}, u32[]{:S(2)}) copy-start(s32[128]{0:T(128)} %param.26) | copy-start | bytes 1540
  6.5 55.8 %all-gather.5.cloned.1.call-start = ((), (), s32[]{:S(2)}) async-start(), calls=%async_computation.3 | async-start | bytes 1179648 | tf_op jit(solution)/shard_map/all_gather | solution.py:97
  38.8 10.0 %copy-start.3 = (bf16[256,1536]{1,0:T(8,128)(2,1)S(1)}, bf16[256,1536]{1,0:T(8,128)(2,1)}, u32[]{:S(2)}) copy-start(bf16[256,1536]{1,0:T(8,128)(2,1)} %param.14) | copy-start | bytes 2359300
  38.8 10.0 %copy-start.10 = (f32[1536]{0:T(1024)S(1)}, f32[1536]{0:T(1024)}, u32[]{:S(2)}) copy-start(f32[1536]{0:T(1024)} %param.15) | copy-start | bytes 18436
  38.8 156.1 %all-to-all-start = ((bf16[16,2,512,256]{3,2,1,0:T(8,128)(2,1)}), bf16[16,2,512,256]{3,2,1,0:T(8,128)(2,1)}, u32[]{:S(2)}, u32[]{:S(2)}) async-start(bf16[16,2,512,256]{3,2,1,0:T(8,128)(2,1)} %copy.33), calls=%async_computation | async-start | bytes 16777216 | tf_op jit(solution)/shard_map/all_to_all | solution.py:116
  47.7 196.4 %all-gather.9.cloned.1.call-start = ((), (), s32[]{:S(2)}) async-start(), calls=%async_computation.5 | async-start | bytes 2088960 | tf_op jit(solution)/shard_map/all_gather | solution.py:131
  48.4 231.0 %all-gather.7.cloned.1.call-start = ((), (), s32[]{:S(2)}) async-start(), calls=%async_computation.4 | async-start | bytes 7077888 | tf_op jit(solution)/shard_map/all_gather | solution.py:129
  74.2 11.4 %copy-start.5 = (bf16[2048,256]{0,1:T(8,128)(2,1)S(1)}, bf16[2048,256]{0,1:T(8,128)(2,1)}, u32[]{:S(2)}) copy-start(bf16[2048,256]{0,1:T(8,128)(2,1)} %all-gather.5.cloned.1.call-done) | copy-start | bytes 3145732
  97.3 106.0 %copy-start.6 = (bf16[1,512,256]{2,1,0:T(8,128)(2,1)S(1)}, bf16[1,512,256]{2,1,0:T(8,128)(2,1)}, u32[]{:S(2)}) copy-start(bf16[1,512,256]{2,1,0:T(8,128)(2,1)} %param.24) | copy-start | bytes 786436
  211.5 19.3 %slice-start = ((s8[4718592]{0:T(1024)(128)(4,1)}), s8[524288]{0:T(1024)(128)(4,1)S(1)}, s32[]{:S(2)}) async-start(s8[4718592]{0:T(1024)(128)(4,1)} %bitcast.59), calls=%async_computation.8 | async-start | bytes 1048576
  222.0 8.8 %slice-start.1 = ((s8[4718592]{0:T(1024)(128)(4,1)}), s8[4194304]{0:T(1024)(128)(4,1)S(1)}, s32[]{:S(2)}) async-start(s8[4718592]{0:T(1024)(128)(4,1)} %bitcast.59), calls=%async_computation.9 | async-start | bytes 8388608
  222.0 8.8 %copy-start.4 = (bf16[256,1536]{1,0:T(8,128)(2,1)S(1)}, bf16[256,1536]{1,0:T(8,128)(2,1)}, u32[]{:S(2)}) copy-start(bf16[256,1536]{1,0:T(8,128)(2,1)} %param.14) | copy-start | bytes 2359300
  230.8 1.5 copy-start.8
  230.8 3.2 copy-start.7
  233.5 91.7 %all-gather.11.cloned.1.call-start = ((), (), s32[]{:S(2)}) async-start(), calls=%async_computation.6 | async-start | bytes 2088960 | tf_op jit(solution)/shard_map/all_gather | solution.py:135
  235.5 53.3 %all-to-all-start.1 = ((bf16[16,96,576]{2,1,0:T(8,128)(2,1)}), bf16[16,96,576]{2,1,0:T(8,128)(2,1)}, u32[]{:S(2)}, u32[]{:S(2)}) async-start(bf16[16,96,576]{2,1,0:T(8,128)(2,1)} %stack.11), calls=%async_computation.1 | async-start | bytes 3932160 | tf_op jit(solution)/shard_map/all_to_all | solution.py:133
  244.0 138.8 %reduce-scatter.2.cloned.1.call-start = ((), (), s32[]{:S(2)}) async-start(), calls=%async_computation.7 | async-start | bytes 7077888 | tf_op jit(solution)/shard_map/reduce_scatter | solution.py:140
  340.8 44.3 %copy-start.1 = (bf16[1536,256]{1,0:T(8,128)(2,1)S(1)}, bf16[1536,256]{1,0:T(8,128)(2,1)}, u32[]{:S(2)}) copy-start(bf16[1536,256]{1,0:T(8,128)(2,1)} %param.17) | copy-start | bytes 2359300
Sparse Core Ops, SparseCore 0:
  20.7 26.9 all-gather.4
  50.7 139.0 all-gather.8
  233.6 45.8 all-gather.6
  281.5 43.6 all-gather.10
  340.9 41.9 reduce-scatter.1
